TPU v7x, 512 devices: a whole 4x4x16 slice. The times are simulated.
512 devices in a mesh: comp: 32 (over z, core), feat: 16 (over x, y).
Axes of the slice: x: 4, y: 4, z: 16, core: 2. Of those that a mesh axis runs over, the one named last changes fastest.
Arguments:
- block_values: bfloat16 [32, 16, 24, 128, 128], P('comp', 'feat'), may hold values from -0.0625 to 0.0625
- block_rows: int32 [32, 16, 24], P('comp', 'feat'), may hold values from 0 to 15, as said below
- block_cols: int32 [32, 16, 24], P('comp', 'feat'), may hold values from 0 to 13, as said below
- block_counts: int32 [32, 16], P('comp', 'feat'), may hold values from 8 to 24, as said below
- right_side: float32 [65536, 128], P(('comp', 'feat')), may hold values from -6 to 6
- ridge: float32 [128], replicated, may hold values from 0.1 to 2
Outputs:
- solution: float32 [28672, 128], P('feat')
- residual: float32 [65536, 128], P(('comp', 'feat'))
Inputs may be any that keep to these rules, and one draw needn't show every extreme that they name: Within one device the listed (block_rows, block_cols) pairs of all 24 slots are distinct; block rows are very uneven in how many blocks they hold. `block_cols`: see block_rows. `block_counts`: slots at or beyond a device's count are ignored; some device is full in every draw.
All inputs are finite; a program needn't handle non-finite values.
Results may differ from a plain program's by a relative error of at most 0.0029.
Values may be sent and summed in bfloat16 or wider, within the bound.
No kernel may reach another device: no remote copies, remote signals or barrier semaphores. Data moves between devices by JAX's collectives and lax.ppermute only.
A program may use at most 64 MiB of HBM per device.

v0:
```python
import jax
import jax.numpy as jnp
from jax import lax
from jax.sharding import PartitionSpec as P

RB_DEV = 16
CB_DEV = 14
ITERS = 2


def shards(block_values, block_rows, block_cols, block_counts, right_side, ridge):
    values = block_values[0, 0]
    slot_rows = block_rows[0, 0]
    slot_cols = block_cols[0, 0]
    count_of_slots = block_counts[0, 0]
    responses = right_side.shape[1]
    total_slot_number = values.shape[0]
    block_edge = values.shape[1]
    slot_live = (jnp.arange(total_slot_number) < count_of_slots).astype(jnp.float32)
    row_lookup_table = (jnp.arange(RB_DEV)[:, None] == slot_rows[None, :]).astype(
        jnp.float32
    ) * slot_live[None, :]
    col_table = (jnp.arange(CB_DEV)[:, None] == slot_cols[None, :]).astype(jnp.float32) * slot_live[
        None, :
    ]
    first_comp = (lax.axis_index("comp") == 0).astype(jnp.float32)

    def backward(low_slab):
        row_slabs = low_slab.reshape(RB_DEV, block_edge, responses)
        selected = jnp.take(row_slabs, slot_rows, axis=0)
        block_products = jnp.einsum(
            "sij,sik->sjk", values, selected, preferred_element_type=jnp.float32
        )
        summed = jnp.einsum(
            "qs,sjk->qjk", col_table, block_products, precision=lax.Precision.HIGHEST
        )
        return summed.reshape(CB_DEV * block_edge, responses)

    residual = right_side
    image_weight = 1.0

    def slab_of(current):
        return lax.all_gather(current.astype(jnp.bfloat16), "feat", axis=0, tiled=True)

    def reduce_grad(partial_contribution):
        return lax.psum(partial_contribution, "comp")

    def grad_total(gradient):
        return lax.psum(first_comp * jnp.sum(gradient * gradient, axis=0), ("comp", "feat"))

    gradient = reduce_grad(backward(slab_of(residual)))
    energy = grad_total(gradient)
    search_direction = gradient
    solution = jnp.zeros_like(gradient)
    for step_index in range(ITERS):
        col_panels = search_direction.astype(jnp.bfloat16).reshape(CB_DEV, block_edge, responses)
        forward_selected = jnp.take(col_panels, slot_cols, axis=0)
        forward_block_products = jnp.einsum(
            "sij,sjk->sik", values, forward_selected, preferred_element_type=jnp.float32
        )
        forward_summed = jnp.einsum(
            "rs,sik->rik", row_lookup_table, forward_block_products, precision=lax.Precision.HIGHEST
        )
        image_rows = lax.psum_scatter(
            forward_summed.reshape(RB_DEV * block_edge, responses),
            "feat",
            scatter_dimension=0,
            tiled=True,
        )
        image_energy, direction_energy = lax.psum(
            (
                image_weight * jnp.sum(image_rows * image_rows, axis=0),
                first_comp * jnp.sum(search_direction * search_direction, axis=0),
            ),
            ("comp", "feat"),
        )
        step_size = energy / (image_energy + ridge * direction_energy)
        solution = solution + step_size * search_direction
        residual = residual - step_size * image_rows
        if step_index + 1 < ITERS:
            gradient = reduce_grad(backward(slab_of(residual))) - ridge * solution
            next_energy = grad_total(gradient)
            search_direction = gradient + next_energy / energy * search_direction
            energy = next_energy
    return (solution, residual)


def solution(mesh):
    placed = (
        P("comp", "feat", None, None, None),
        P("comp", "feat", None),
        P("comp", "feat", None),
        P("comp", "feat"),
        P(("comp", "feat"), None),
        P(),
    )
    return jax.shard_map(
        shards,
        mesh=mesh,
        in_specs=placed,
        out_specs=(P("feat", None), P(("comp", "feat"), None)),
        check_vma=False,
    )
```

profile of v0, /device:TPU:1, one launch (start us, length us, event | category | flops | bytes accessed | tf_op | source)
XLA Modules:
  0.0 996.0 jit_solution(15830034595637753856)
XLA Ops:
  7.2 0.0 copy-start
  7.2 0.0 all-reduce.5.cloned.1.call-start
  7.2 0.7 compare_and_fusion.1
  8.0 0.7 compare_select_fusion.1
  9.3 0.8 convert_element_type.26
  10.1 20.0 %all_gather.6 = bf16[2048,128]{1,0:T(8,128)(2,1)S(1)} all-gather(bf16[128,128]{1,0:T(8,128)(2,1)S(1)} %convert_element_type.26), channel_id=1, replica_groups=mesh['comp'=32,'feat'=16] {'feat'}, dimensions={0}, use_global_device_ids=true | all-gather | bytes 557056 | tf_op jit(solution)/shard_map/all_gather | solution.py:43
  30.1 0.7 gather_fusion
  30.8 0.0 copy-done
  30.8 1.7 fusion.14
  32.5 0.0 copy-start.7
  32.5 2.0 copy.12
  34.5 0.0 copy-done.7
  34.5 1.0 fusion.6
  35.5 1.2 copy.8
  36.7 0.0 all-reduce.5.cloned.1.call-update
  36.7 0.0 reduce-scatter.3.cloned.1.call-start
  36.8 213.7 %all-reduce.5.cloned.1.call-done = f32[1792,128]{1,0:T(8,128)} async-done(((f32[1792,128]{1,0:T(8,128)}), f32[1792,128]{1,0:T(8,128)}) %all-reduce.5.cloned.1.call-update) | async-done | bytes 917520 | tf_op jit(solution)/shard_map/psum | solution.py:46
  250.5 1.7 multiply_reduce_fusion.2
  252.3 0.7 gather_fusion.1
  253.0 2.0 fusion.12
  255.0 0.0 copy-start.8
  255.0 2.0 copy.13
  256.9 0.0 copy-done.8
  257.0 1.0 fusion.4
  258.0 0.0 copy-start.6
  258.0 0.0 copy-start.3
  258.0 1.3 copy.9
  259.3 0.0 reduce-scatter.3.cloned.1.call-update
  259.3 0.0 all-reduce.7.cloned.1.call-start
  259.4 86.1 %reduce-scatter.3.cloned.1.call-done = f32[128,128]{1,0:T(8,128)} async-done(((f32[2048,128]{1,0:T(8,128)}), f32[128,128]{1,0:T(8,128)}) %reduce-scatter.3.cloned.1.call-update) | async-done | bytes 65552 | tf_op jit(solution)/shard_map/reduce_scatter | solution.py:64
  345.5 0.9 multiply_reduce_fusion.4
  346.3 105.3 %all-reduce.1 = (f32[128]{0:T(128)S(1)}, f32[128]{0:T(128)S(1)}) all-reduce(f32[128]{0:T(128)S(1)} %broadcast_multiply_fusion.2, f32[128]{0:T(128)S(1)} %multiply_reduce_fusion.4), channel_id=1, replica_groups=mesh['comp'=32,'feat'=16] {'comp','feat'}, use_global_device_ids=true, to_apply=%region_2.4 | all-reduce | flops 256 | bytes 2048 | tf_op jit(solution)/shard_map/psum | solution.py:49
  451.6 0.0 copy-done.6
  451.6 0.0 copy-done.3
  451.6 0.9 fusion.28
  452.5 16.0 %all_gather.7 = bf16[2048,128]{1,0:T(8,128)(2,1)S(1)} all-gather(bf16[128,128]{1,0:T(8,128)(2,1)S(1)} %fusion.28), channel_id=1, replica_groups=mesh['comp'=32,'feat'=16] {'feat'}, dimensions={0}, use_global_device_ids=true | all-gather | bytes 557056 | tf_op jit(solution)/shard_map/all_gather | solution.py:43
  468.5 0.7 gather_fusion.2
  469.2 1.7 fusion.10
  470.9 2.0 copy.14
  472.9 1.0 fusion.2
  473.9 0.0 copy-start.1
  473.9 1.2 copy.10
  475.1 0.0 all-reduce.7.cloned.1.call-update
  475.1 0.0 reduce-scatter.5.cloned.1.call-start
  475.2 208.0 %all-reduce.7.cloned.1.call-done = f32[1792,128]{1,0:T(8,128)} async-done(((f32[1792,128]{1,0:T(8,128)}), f32[1792,128]{1,0:T(8,128)}) %all-reduce.7.cloned.1.call-update) | async-done | bytes 917520 | tf_op jit(solution)/shard_map/psum | solution.py:46
  683.2 0.0 copy-done.1
  683.2 1.5 multiply_reduce_fusion.1
  684.7 105.2 %psum.56 = f32[128]{0:T(128)S(1)} all-reduce(f32[128]{0:T(128)S(1)} %broadcast_multiply_fusion.1), channel_id=1, replica_groups=mesh['comp'=32,'feat'=16] {'comp','feat'}, use_global_device_ids=true, to_apply=%region_8.11 | all-reduce | flops 128 | bytes 1024 | tf_op jit(solution)/shard_map/psum | solution.py:49
  789.9 0.0 copy-done.2
  789.9 0.3 multiply_reduce_fusion
  790.2 1.6 gather_fusion.3
  791.7 3.1 fusion.8
  794.8 3.0 copy.15
  797.9 2.4 fusion
  800.3 1.3 copy.11
  801.6 0.0 reduce-scatter.5.cloned.1.call-update
  801.6 0.0 copy-start.4
  801.6 79.8 %reduce-scatter.5.cloned.1.call-done = f32[128,128]{1,0:T(8,128)} async-done(((f32[2048,128]{1,0:T(8,128)}), f32[128,128]{1,0:T(8,128)}) %reduce-scatter.5.cloned.1.call-update) | async-done | bytes 65552 | tf_op jit(solution)/shard_map/reduce_scatter | solution.py:64
  881.5 0.9 multiply_reduce_fusion.3
  882.4 105.3 %all-reduce = (f32[128]{0:T(128)S(1)}, f32[128]{0:T(128)S(1)}) all-reduce(f32[128]{0:T(128)S(1)} %multiply_reduce_fusion.3, f32[128]{0:T(128)S(1)} %broadcast_multiply_fusion), channel_id=1, replica_groups=mesh['comp'=32,'feat'=16] {'comp','feat'}, use_global_device_ids=true, to_apply=%region_11.14 | all-reduce | flops 256 | bytes 2048 | tf_op jit(solution)/shard_map/psum | solution.py:70
  987.7 1.1 multiply_add_fusion
  988.8 0.0 copy-done.4
  988.8 0.0 copy-done.5
  988.8 0.6 multiply_subtract_fusion.1
  (13 shorter events, 0.1 us)
Async XLA Ops:
  7.2 23.6 %copy-start = (bf16[1,1,24,128,128]{4,3,2,1,0:T(8,128)(2,1)S(1)}, bf16[1,1,24,128,128]{4,3,2,1,0:T(8,128)(2,1)}, u32[]{:S(2)}) copy-start(bf16[1,1,24,128,128]{4,3,2,1,0:T(8,128)(2,1)} %param.10) | copy-start | bytes 2359300
  7.2 243.4 %all-reduce.5.cloned.1.call-start = ((), (), s32[]{:S(2)}) async-start(), calls=%async_computation.2 | async-start | bytes 1835008 | tf_op jit(solution)/shard_map/psum | solution.py:46
  32.5 2.0 copy-start.7
  36.7 308.8 %reduce-scatter.3.cloned.1.call-start = ((), (), s32[]{:S(2)}) async-start(), calls=%async_computation.3 | async-start | bytes 1114112 | tf_op jit(solution)/shard_map/reduce_scatter | solution.py:64
  255.0 2.0 copy-start.8
  258.0 193.6 %copy-start.6 = (f32[128]{0:T(128)S(1)}, f32[128]{0:T(128)}, u32[]{:S(2)}) copy-start(f32[128]{0:T(128)} %param.15) | copy-start | bytes 1540
  258.0 193.6 %copy-start.3 = (f32[128,128]{1,0:T(8,128)S(1)}, f32[128,128]{1,0:T(8,128)}, u32[]{:S(2)}) copy-start(f32[128,128]{1,0:T(8,128)} %param.14) | copy-start | bytes 196612
  259.3 423.9 %all-reduce.7.cloned.1.call-start = ((), (), s32[]{:S(2)}) async-start(), calls=%async_computation.4 | async-start | bytes 1835008 | tf_op jit(solution)/shard_map/psum | solution.py:46
  473.9 209.3 %copy-start.1 = (f32[1792,128]{1,0:T(8,128)S(1)}, f32[1792,128]{1,0:T(8,128)}, u32[]{:S(2)}) copy-start(f32[1792,128]{1,0:T(8,128)} %all-reduce.5.cloned.1.call-done) | copy-start | bytes 2752516
  475.1 406.3 %reduce-scatter.5.cloned.1.call-start = ((), (), s32[]{:S(2)}) async-start(), calls=%async_computation.5 | async-start | bytes 1114112 | tf_op jit(solution)/shard_map/reduce_scatter | solution.py:64
  683.2 106.7 %copy-start.2 = (f32[1792,128]{1,0:T(8,128)S(1)}, f32[1792,128]{1,0:T(8,128)}, u32[]{:S(2)}) copy-start(f32[1792,128]{1,0:T(8,128)} %all-reduce.7.cloned.1.call-done) | copy-start | bytes 2752516
  801.6 187.2 %copy-start.4 = (f32[128,128]{1,0:T(8,128)S(1)}, f32[128,128]{1,0:T(8,128)}, u32[]{:S(2)}) copy-start(f32[128,128]{1,0:T(8,128)} %reduce-scatter.3.cloned.1.call-done) | copy-start | bytes 196612
  881.4 107.4 %copy-start.5 = (f32[128,128]{1,0:T(8,128)S(1)}, f32[128,128]{1,0:T(8,128)}, u32[]{:S(2)}) copy-start(f32[128,128]{1,0:T(8,128)} %reduce-scatter.5.cloned.1.call-done) | copy-start | bytes 196612
Sparse Core Ops, SparseCore 0:
  36.8 213.6 all-reduce.4
  259.5 85.9 reduce-scatter.2
  475.3 207.9 all-reduce.6
  801.7 79.6 reduce-scatter.4
where the time goes:
time: 997 us; the launch traced here: 996 us
  waiting for transfers between devices  588 us (59%)
  blocking collectives  352 us (35%)
  local copies, waits for them, and re-layouts  17.6 us (2%)
  between operations  14.6 us (1%)
  matrix products  13.9 us (1%)
  other arithmetic  10.2 us (1%)
    psum x2, waiting for transfers between devices, reduce_grad(): return lax.psum(partial_contribution, 'comp')  422 us
    psum x2, blocking collectives, grad_total(): lax.psum(first_comp * jnp.sum(gradient * gradient, axis=0), ('comp', 'fea...  210 us
    reduce_scatter x2, waiting for transfers between devices, shards(): lax.psum_scatter(forward_summed.reshape(RB_DEV * block_edge, responses),...  166 us
    psum x1, blocking collectives, shards(): lax.psum((image_weight * jnp.sum(image_rows * image_rows, axis=0), first_...  105 us
    all_gather x2, blocking collectives, slab_of(): lax.all_gather(current.astype(jnp.bfloat16), 'feat', axis=0, tiled=True)  36 us
  transfers between devices with their start and end apart: 4, of which 4 were waited for; matrix products, arithmetic and copies ran while one was open for 0% of the time, Pallas kernels for 0%

commit v1 on v0

--- a/solution.py
+++ b/solution.py
@@ -46,7 +46,10 @@
         return lax.psum(partial_contribution, "comp")
 
     def grad_total(gradient):
-        return lax.psum(first_comp * jnp.sum(gradient * gradient, axis=0), ("comp", "feat"))
+        return jnp.sum(
+            lax.all_gather(first_comp * jnp.sum(gradient * gradient, axis=0), ("comp", "feat")),
+            axis=0,
+        )
 
     gradient = reduce_grad(backward(slab_of(residual)))
     energy = grad_total(gradient)

time: 997 us -> 1160 us (1.16)
  blocking collectives: 352 us -> 598 us
  waiting for transfers between devices: 588 us -> 505 us
    all_gather x0 -> x2, blocking collectives: none -> 352 us  [grad_total(): lax.all_gather(first_comp * jnp.sum(gradient * gradient, axis=0), ('comp'...]
    psum x2 -> x0, blocking collectives: 210 us -> none  [grad_total(): lax.psum(first_comp * jnp.sum(gradient * gradient, axis=0), ('comp', 'fea...]
    psum x1 -> x2, blocking collectives: 105 us -> 209 us  [shards(): lax.psum((image_weight * jnp.sum(image_rows * image_rows, axis=0), first_...]
    reduce_scatter x2, waiting for transfers between devices: 166 us -> 85.1 us  [shards(): lax.psum_scatter(forward_summed.reshape(RB_DEV * block_edge, responses),...]
  transfers between devices with their start and end apart: 4 -> 4, of which waited for: 4 -> 3; matrix products, arithmetic and copies ran while one was open for 0% -> 0% of each run, Pallas kernels for 0% -> 0%
where the time goes in v1:
time: 1160 us
  blocking collectives  598 us (52%)
  waiting for transfers between devices  505 us (44%)
  local copies, waits for them, and re-layouts  17.6 us (2%)
  between operations  14.7 us (1%)
  matrix products  13.9 us (1%)
    psum x2, waiting for transfers between devices, reduce_grad(): return lax.psum(partial_contribution, 'comp')  420 us
    all_gather x2, blocking collectives, grad_total(): lax.all_gather(first_comp * jnp.sum(gradient * gradient, axis=0), ('comp'...  352 us
    psum x2, blocking collectives, shards(): lax.psum((image_weight * jnp.sum(image_rows * image_rows, axis=0), first_...  209 us
    reduce_scatter x2, waiting for transfers between devices, shards(): lax.psum_scatter(forward_summed.reshape(RB_DEV * block_edge, responses),...  85.1 us
    all_gather x2, blocking collectives, slab_of(): lax.all_gather(current.astype(jnp.bfloat16), 'feat', axis=0, tiled=True)  36.4 us
  transfers between devices with their start and end apart: 4, of which 3 were waited for; matrix products, arithmetic and copies ran while one was open for 0% of the time, Pallas kernels for 0%

profile of v1, /device:TPU:1, one launch (start us, length us, event | category | flops | bytes accessed | tf_op | source)
XLA Modules:
  0.0 1160.5 jit_solution(7649192751832702972)
XLA Ops:
  7.2 0.0 copy-start
  7.2 0.0 all-reduce.5.cloned.1.call-start
  7.2 0.7 compare_and_fusion.1
  8.0 0.7 compare_select_fusion.1
  9.3 0.8 convert_element_type.26
  10.1 20.0 %all_gather.14 = bf16[2048,128]{1,0:T(8,128)(2,1)S(1)} all-gather(bf16[128,128]{1,0:T(8,128)(2,1)S(1)} %convert_element_type.26), channel_id=1, replica_groups=mesh['comp'=32,'feat'=16] {'feat'}, dimensions={0}, use_global_device_ids=true | all-gather | bytes 557056 | tf_op jit(solution)/shard_map/all_gather | solution.py:43
  30.1 0.7 gather_fusion
  30.8 0.0 copy-done
  30.8 1.7 convolution_bitcast_fusion.3
  32.5 2.0 copy.21
  34.5 0.0 copy-done.7
  34.5 1.0 fusion.25
  35.5 1.2 copy.22
  36.7 0.0 all-reduce.5.cloned.1.call-update
  36.7 0.0 reduce-scatter.3.cloned.1.call-start
  36.8 213.7 %all-reduce.5.cloned.1.call-done = f32[1792,128]{1,0:T(8,128)} async-done(((f32[1792,128]{1,0:T(8,128)}), f32[1792,128]{1,0:T(8,128)}) %all-reduce.5.cloned.1.call-update) | async-done | bytes 917520 | tf_op jit(solution)/shard_map/psum | solution.py:46
  250.5 1.7 multiply_reduce_fusion.2
  252.3 0.7 gather_fusion.1
  253.0 2.0 convolution_bitcast_fusion.2
  255.0 2.0 copy.24
  256.9 0.0 copy-done.8
  257.0 1.0 fusion.19
  258.0 0.0 copy-start.6
  258.0 0.0 copy-start.3
  258.0 1.3 copy.25
  259.3 0.0 reduce-scatter.3.cloned.1.call-update
  259.3 0.0 all-reduce.7.cloned.1.call-start
  259.4 179.0 %all-gather.2 = f32[512,1,128]{2,1,0:T(1,128)S(1)} all-gather(f32[1,1,128]{2,1,0:T(1,128)S(1)} %fusion.54), channel_id=2, replica_groups=mesh['comp'=32,'feat'=16] {'comp','feat'}, dimensions={0}, use_global_device_ids=true | all-gather | bytes 262656 | tf_op jit(solution)/shard_map/all_gather | solution.py:50
  438.4 0.6 reduce_sum.68
  439.0 0.0 reduce-scatter.3.cloned.1.call-done
  439.0 0.9 multiply_reduce_fusion.4
  439.9 103.6 %all-reduce.1 = (f32[128]{0:T(128)S(1)}, f32[128]{0:T(128)S(1)}) all-reduce(f32[128]{0:T(128)S(1)} %multiply_reduce_fusion.4, f32[128]{0:T(128)S(1)} %broadcast_multiply_fusion.1), channel_id=1, replica_groups=mesh['comp'=32,'feat'=16] {'comp','feat'}, use_global_device_ids=true, to_apply=%region_5.8 | all-reduce | flops 256 | bytes 2048 | tf_op jit(solution)/shard_map/psum | solution.py:73
  543.4 0.0 copy-done.6
  543.5 0.0 copy-done.3
  543.5 0.9 fusion.16
  544.3 16.4 %all_gather.16 = bf16[2048,128]{1,0:T(8,128)(2,1)S(1)} all-gather(bf16[128,128]{1,0:T(8,128)(2,1)S(1)} %fusion.16), channel_id=1, replica_groups=mesh['comp'=32,'feat'=16] {'feat'}, dimensions={0}, use_global_device_ids=true | all-gather | bytes 557056 | tf_op jit(solution)/shard_map/all_gather | solution.py:43
  560.8 0.7 gather_fusion.2
  561.5 1.7 convolution_bitcast_fusion.1
  563.1 2.0 copy.27
  565.1 1.0 fusion.23
  566.1 0.0 copy-start.1
  566.1 1.2 copy.28
  567.3 0.0 all-reduce.7.cloned.1.call-update
  567.3 0.0 reduce-scatter.5.cloned.1.call-start
  567.4 206.2 %all-reduce.7.cloned.1.call-done = f32[1792,128]{1,0:T(8,128)} async-done(((f32[1792,128]{1,0:T(8,128)}), f32[1792,128]{1,0:T(8,128)}) %all-reduce.7.cloned.1.call-update) | async-done | bytes 917520 | tf_op jit(solution)/shard_map/psum | solution.py:46
  773.6 0.0 copy-done.1
  773.6 1.5 multiply_reduce_fusion.1
  775.1 173.3 %all-gather.3 = f32[512,1,128]{2,1,0:T(1,128)S(1)} all-gather(f32[1,1,128]{2,1,0:T(1,128)S(1)} %multiply_bitcast_fusion), channel_id=3, replica_groups=mesh['comp'=32,'feat'=16] {'comp','feat'}, dimensions={0}, use_global_device_ids=true | all-gather | bytes 262656 | tf_op jit(solution)/shard_map/all_gather | solution.py:50
  948.4 0.6 reduce_sum.71
  949.0 0.0 copy-done.2
  949.0 0.3 multiply_reduce_fusion
  949.3 1.6 gather_fusion.3
  950.8 3.1 convolution_bitcast_fusion
  954.0 3.0 copy.30
  957.0 2.4 fusion.17
  959.4 1.3 copy.31
  960.7 0.0 reduce-scatter.5.cloned.1.call-update
  960.7 0.0 copy-start.4
  960.8 85.1 %reduce-scatter.5.cloned.1.call-done = f32[128,128]{1,0:T(8,128)} async-done(((f32[2048,128]{1,0:T(8,128)}), f32[128,128]{1,0:T(8,128)}) %reduce-scatter.5.cloned.1.call-update) | async-done | bytes 65552 | tf_op jit(solution)/shard_map/reduce_scatter | solution.py:67
  1045.9 0.9 multiply_reduce_fusion.3
  1046.8 105.3 %all-reduce = (f32[128]{0:T(128)S(1)}, f32[128]{0:T(128)S(1)}) all-reduce(f32[128]{0:T(128)S(1)} %multiply_reduce_fusion.3, f32[128]{0:T(128)S(1)} %broadcast_multiply_fusion), channel_id=1, replica_groups=mesh['comp'=32,'feat'=16] {'comp','feat'}, use_global_device_ids=true, to_apply=%region_12.15 | all-reduce | flops 256 | bytes 2048 | tf_op jit(solution)/shard_map/psum | solution.py:73
  1152.2 1.1 multiply_add_fusion
  1153.3 0.0 copy-done.4
  1153.3 0.6 multiply_subtract_fusion.1
  (17 shorter events, 0.1 us)
Async XLA Ops:
  7.2 23.6 %copy-start = (bf16[1,1,24,128,128]{4,3,2,1,0:T(8,128)(2,1)S(1)}, bf16[1,1,24,128,128]{4,3,2,1,0:T(8,128)(2,1)}, u32[]{:S(2)}) copy-start(bf16[1,1,24,128,128]{4,3,2,1,0:T(8,128)(2,1)} %param.10) | copy-start | bytes 2359300
  7.2 243.4 %all-reduce.5.cloned.1.call-start = ((), (), s32[]{:S(2)}) async-start(), calls=%async_computation.2 | async-start | bytes 1835008 | tf_op jit(solution)/shard_map/psum | solution.py:46
  32.5 2.0 copy-start.7
  36.7 402.3 %reduce-scatter.3.cloned.1.call-start = ((), (), s32[]{:S(2)}) async-start(), calls=%async_computation.3 | async-start | bytes 1114112 | tf_op jit(solution)/shard_map/reduce_scatter | solution.py:67
  255.0 2.0 copy-start.8
  258.0 285.5 %copy-start.6 = (f32[128]{0:T(128)S(1)}, f32[128]{0:T(128)}, u32[]{:S(2)}) copy-start(f32[128]{0:T(128)} %param.15) | copy-start | bytes 1540
  258.0 285.5 %copy-start.3 = (f32[128,128]{1,0:T(8,128)S(1)}, f32[128,128]{1,0:T(8,128)}, u32[]{:S(2)}) copy-start(f32[128,128]{1,0:T(8,128)} %param.14) | copy-start | bytes 196612
  259.3 514.2 %all-reduce.7.cloned.1.call-start = ((), (), s32[]{:S(2)}) async-start(), calls=%async_computation.4 | async-start | bytes 1835008 | tf_op jit(solution)/shard_map/psum | solution.py:46
  566.1 207.5 %copy-start.1 = (f32[1792,128]{1,0:T(8,128)S(1)}, f32[1792,128]{1,0:T(8,128)}, u32[]{:S(2)}) copy-start(f32[1792,128]{1,0:T(8,128)} %all-reduce.5.cloned.1.call-done) | copy-start | bytes 2752516
  567.3 478.5 %reduce-scatter.5.cloned.1.call-start = ((), (), s32[]{:S(2)}) async-start(), calls=%async_computation.5 | async-start | bytes 1114112 | tf_op jit(solution)/shard_map/reduce_scatter | solution.py:67
  773.6 175.4 %copy-start.2 = (f32[1792,128]{1,0:T(8,128)S(1)}, f32[1792,128]{1,0:T(8,128)}, u32[]{:S(2)}) copy-start(f32[1792,128]{1,0:T(8,128)} %all-reduce.7.cloned.1.call-done) | copy-start | bytes 2752516
  960.7 192.5 %copy-start.4 = (f32[128,128]{1,0:T(8,128)S(1)}, f32[128,128]{1,0:T(8,128)}, u32[]{:S(2)}) copy-start(f32[128,128]{1,0:T(8,128)} %reduce-scatter.3.cloned.1.call-done) | copy-start | bytes 196612
  1045.9 107.4 %copy-start.5 = (f32[128,128]{1,0:T(8,128)S(1)}, f32[128,128]{1,0:T(8,128)}, u32[]{:S(2)}) copy-start(f32[128,128]{1,0:T(8,128)} %reduce-scatter.5.cloned.1.call-done) | copy-start | bytes 196612
Sparse Core Ops, SparseCore 0:
  36.8 213.6 all-reduce.4
  259.5 85.9 reduce-scatter.2
  567.5 206.0 all-reduce.6
  960.9 84.9 reduce-scatter.4
